TPU v7x, 32 devices: a whole 2x2x4 slice. The times are simulated.
32 devices in a mesh: real: 2 (over x), los: 8 (over z, y), sky: 2 (over core).
Axes of the slice: x: 2, y: 2, z: 4, core: 2. Of those that a mesh axis runs over, the one named last changes fastest.
Arguments:
- density: float32 [16, 2048, 2048], P(('real', 'los'), 'sky'), parts along dimension 0, may hold values from -6 to 8
- lens_weight: float32 [16], P(('real', 'los')), parts along dimension 0, may hold values from 0.05 to 0.4
- plane_count: int32 [16], P(('real', 'los')), parts along dimension 0, may hold values from 0 to 1
- ray_state: float32 [16, 12, 32, 2048], P(('real', 'los'), None, 'sky'), parts along dimension 0, may hold values from -6 to 6
Outputs:
- ray_out: float32 [16, 12, 32, 2048], P(('real', 'los'), None, 'sky'), parts along dimension 0
There are 2 independent parts, one for each index of `real`. A program takes and returns all parts, laid end to end along the dimension named above; each array names one. Nothing has to cross between parts.
All inputs are finite; a program needn't handle non-finite values.
Results may differ from a plain program's by a relative error of at most 0.00012.
Values sent between devices are 32-bit elements; how exact they have to be, the bound alone decides.
No kernel may reach another device: no remote copies, remote signals or barrier semaphores. Data moves between devices by JAX's collectives and lax.ppermute only.
A program may use at most 128 MiB of HBM per device.

v0:
```python
import math
import jax
import jax.numpy as jnp
from jax import lax
from jax.sharding import PartitionSpec as P

HOPS = 4
two_pi = 2.0 * math.pi
highest = lax.Precision.HIGHEST
first_radix = 16


def shifted(block, axis, distance):
    devices = range(lax.axis_size(axis))
    route = [((i - distance) % len(devices), i) for i in devices]
    return lax.ppermute(block, axis, route)


def lens_step(ray_tile, fields):
    disp_x = ray_tile[..., 0, :, :]
    disp_y = ray_tile[..., 1, :, :]
    tilt_x = ray_tile[..., 2, :, :]
    tilt_y = ray_tile[..., 3, :, :]
    jac_xx = ray_tile[..., 4, :, :]
    jac_xy = ray_tile[..., 5, :, :]
    jac_yx = ray_tile[..., 6, :, :]
    jac_yy = ray_tile[..., 7, :, :]
    rate_xx = ray_tile[..., 8, :, :]
    rate_xy = ray_tile[..., 9, :, :]
    rate_yx = ray_tile[..., 10, :, :]
    rate_yy = ray_tile[..., 11, :, :]
    bend_x = fields[..., 0, :, :]
    bend_y = fields[..., 1, :, :]
    hess_xx = fields[..., 2, :, :]
    hess_yy = fields[..., 3, :, :]
    hess_xy = fields[..., 4, :, :]
    push_x = bend_x + hess_xx * disp_x + hess_xy * disp_y
    push_y = bend_y + hess_xy * disp_x + hess_yy * disp_y
    new_tilt_x = tilt_x - push_x
    new_tilt_y = tilt_y - push_y
    new_disp_x = disp_x + new_tilt_x
    new_disp_y = disp_y + new_tilt_y
    new_rate_xx = rate_xx - (hess_xx * jac_xx + hess_xy * jac_yx)
    new_rate_xy = rate_xy - (hess_xx * jac_xy + hess_xy * jac_yy)
    new_rate_yx = rate_yx - (hess_xy * jac_xx + hess_yy * jac_yx)
    new_rate_yy = rate_yy - (hess_xy * jac_xy + hess_yy * jac_yy)
    new_jac_xx = jac_xx + new_rate_xx
    new_jac_xy = jac_xy + new_rate_xy
    new_jac_yx = jac_yx + new_rate_yx
    new_jac_yy = jac_yy + new_rate_yy
    return jnp.stack(
        [
            new_disp_x,
            new_disp_y,
            new_tilt_x,
            new_tilt_y,
            new_jac_xx,
            new_jac_xy,
            new_jac_yx,
            new_jac_yy,
            new_rate_xx,
            new_rate_xy,
            new_rate_yx,
            new_rate_yy,
        ],
        axis=-3,
    )


def phase_table(left_idx, right_idx, modulus, orient):
    product = left_idx[:, None] * right_idx[None, :] % modulus
    angle = orient * two_pi / modulus * product.astype(jnp.float32)
    return (jnp.cos(angle), jnp.sin(angle))


def mixed(form, left_op, right_op):
    return jnp.einsum(
        form, left_op, right_op, precision=highest, preferred_element_type=jnp.float32
    )


def complex_product(form, real_in, imag_in, table_re, table_im):
    if imag_in is None:
        return (mixed(form, real_in, table_re), mixed(form, real_in, table_im))
    out_re = mixed(form, real_in, table_re) - mixed(form, imag_in, table_im)
    out_im = mixed(form, real_in, table_im) + mixed(form, imag_in, table_re)
    return (out_re, out_im)


def first_factor_of(length):
    factor_one = 1
    while factor_one * factor_one < length and length % (factor_one * 2) == 0:
        factor_one = factor_one * 2
    return factor_one


def rows_forward(cells, k_count, m_count):
    row_count, length = cells.shape
    second = length // first_radix
    shaped = cells.reshape(row_count, first_radix, second)
    v_idx = jnp.arange(first_radix, dtype=jnp.int32)
    k_idx = jnp.arange(k_count, dtype=jnp.int32)
    u_idx = jnp.arange(second, dtype=jnp.int32)
    m_idx = jnp.arange(m_count, dtype=jnp.int32)
    section_re, section_im = phase_table(v_idx, k_idx, first_radix, -1.0)
    part_re, part_im = complex_product("rvu,vk->rku", shaped, None, section_re, section_im)
    twist_re, twist_im = phase_table(k_idx, u_idx, length, -1.0)
    turned_re = part_re * twist_re - part_im * twist_im
    turned_im = part_re * twist_im + part_im * twist_re
    final_re, final_im = phase_table(u_idx, m_idx, second, -1.0)
    done_re, done_im = complex_product("rku,um->rkm", turned_re, turned_im, final_re, final_im)
    return (
        done_re.reshape(row_count, k_count * m_count),
        done_im.reshape(row_count, k_count * m_count),
    )


def rows_inverse(spec_re, spec_im, length, m_count):
    row_count = spec_re.shape[0]
    second = length // first_radix
    shaped_re = spec_re.reshape(row_count, first_radix, m_count)
    shaped_im = spec_im.reshape(row_count, first_radix, m_count)
    k_idx = jnp.arange(first_radix, dtype=jnp.int32)
    u_idx = jnp.arange(second, dtype=jnp.int32)
    m_idx = jnp.arange(m_count, dtype=jnp.int32)
    section_re, section_im = phase_table(m_idx, u_idx, second, 1.0)
    part_re, part_im = complex_product("rkm,mu->rku", shaped_re, shaped_im, section_re, section_im)
    twist_re, twist_im = phase_table(k_idx, u_idx, length, 1.0)
    turned_re = part_re * twist_re - part_im * twist_im
    turned_im = part_re * twist_im + part_im * twist_re
    final_re, final_im = phase_table(k_idx, k_idx, first_radix, 1.0)
    done_re, done_im = complex_product("rku,kv->rvu", turned_re, turned_im, final_re, final_im)
    return (done_re.reshape(row_count, length), done_im.reshape(row_count, length))


def transform_first(real_in, imag_in, orient):
    length, col_count = real_in.shape
    factor_one = first_factor_of(length)
    second = length // factor_one
    shaped_re = real_in.reshape(factor_one, second, col_count)
    shaped_im = imag_in.reshape(factor_one, second, col_count)
    first_idx = jnp.arange(factor_one, dtype=jnp.int32)
    second_idx = jnp.arange(second, dtype=jnp.int32)
    section_re, section_im = phase_table(first_idx, first_idx, factor_one, orient)
    part_re, part_im = complex_product("abc,ak->kbc", shaped_re, shaped_im, section_re, section_im)
    twist_re, twist_im = phase_table(first_idx, second_idx, length, orient)
    twist_re = twist_re[:, :, None]
    twist_im = twist_im[:, :, None]
    turned_re = part_re * twist_re - part_im * twist_im
    turned_im = part_re * twist_im + part_im * twist_re
    final_re, final_im = phase_table(second_idx, second_idx, second, orient)
    done_re, done_im = complex_product("kbc,bm->mkc", turned_re, turned_im, final_re, final_im)
    return (done_re.reshape(length, col_count), done_im.reshape(length, col_count))


def wavenumbers(indices, length):
    signed = jnp.where(indices < length // 2, indices, indices - length)
    return (two_pi / length * signed.astype(jnp.float32), indices != length // 2)


def poisson_kernel(wave_row, retain_row, wave_col, retain_col, norm_factor):
    squared = wave_col * wave_col + wave_row * wave_row
    retain = retain_row & retain_col & (squared > 0.0)
    safe_sq = jnp.where(retain, squared, 1.0)
    return jnp.where(retain, -2.0 / (safe_sq * norm_factor), 0.0)


def half_spectra(
    piece_re, piece_im, wave_row, retain_row, wave_col, retain_col, col_idx, norm_factor
):
    kernel = poisson_kernel(wave_row, retain_row, wave_col, retain_col, norm_factor)
    weight = jnp.where(col_idx == 0, 1.0, 2.0).astype(jnp.float32)
    phi_re = kernel * weight * piece_re
    phi_im = kernel * weight * piece_im
    cross_term = wave_col * wave_row
    col_sq = wave_col * wave_col
    row_sq = wave_row * wave_row
    all_re = [
        -wave_col * phi_im,
        -wave_row * phi_im,
        -col_sq * phi_re,
        -row_sq * phi_re,
        -cross_term * phi_re,
    ]
    all_im = [
        wave_col * phi_re,
        wave_row * phi_re,
        -col_sq * phi_im,
        -row_sq * phi_im,
        -cross_term * phi_im,
    ]
    return (jnp.stack(all_re), jnp.stack(all_im))


def spectral_rows(spec_re, spec_im, col_begin, ray_all, stride, maker, count, m_count):
    length, col_count = spec_re.shape
    block_cols = min(col_count, 256)
    blocks = col_count // block_cols
    freq_idx = jnp.arange(length, dtype=jnp.int32)
    wave_row, retain_row = wavenumbers(freq_idx, length)
    ray_idx = jnp.arange(ray_all, dtype=jnp.int32) * stride
    back_re, back_im = phase_table(ray_idx, freq_idx, length, 1.0)
    norm_factor = float(length * length)

    def one_block(block_index, result):
        offset = block_index * block_cols
        piece_re = lax.dynamic_slice_in_dim(spec_re, offset, block_cols, 1)
        piece_im = lax.dynamic_slice_in_dim(spec_im, offset, block_cols, 1)
        position = col_begin + offset + jnp.arange(block_cols, dtype=jnp.int32)
        col_idx = first_radix * (position % m_count) + position // m_count
        wave_col, retain_col = wavenumbers(col_idx, length)
        packed_re, packed_im = maker(
            piece_re,
            piece_im,
            wave_row[:, None],
            retain_row[:, None],
            wave_col[None, :],
            retain_col[None, :],
            col_idx[None, :],
            norm_factor,
        )
        out_re, out_im = complex_product("fkc,rk->frc", packed_re, packed_im, back_re, back_im)
        return lax.dynamic_update_slice_in_dim(
            result, jnp.stack([out_re, out_im], axis=1), offset, 3
        )

    initial = jnp.zeros((count, 2, ray_all, col_count), jnp.float32)
    return lax.fori_loop(0, blocks, one_block, initial)


def per_device(density, lens_weight, plane_count, ray_state):
    sky_count = lax.axis_size("sky")
    sky_index = lax.axis_index("sky")
    plane_cells = density[0]
    length = plane_cells.shape[1]
    second = length // first_radix
    ray_dev = ray_state.shape[2]
    ray_all = ray_dev * sky_count
    stride = length // ray_all
    strength = lens_weight[0] * plane_count[0].astype(jnp.float32)
    back_count = second // 2
    row_re, row_im = rows_forward(plane_cells, first_radix, back_count)
    spread = lax.all_to_all(
        jnp.stack([row_re, row_im]), "sky", split_axis=2, concat_axis=1, tiled=True
    )
    spec_re, spec_im = transform_first(spread[0], spread[1], -1.0)
    half_count = length // (2 * sky_count)
    packed = spectral_rows(
        spec_re, spec_im, sky_index * half_count, ray_all, stride, half_spectra, 5, back_count
    )
    returned = lax.all_to_all(packed, "sky", split_axis=2, concat_axis=3, tiled=True)
    count = returned.shape[0]
    width_in = returned.shape[3]
    flat_re = returned[:, 0].reshape(count * ray_dev, width_in)
    flat_im = returned[:, 1].reshape(count * ray_dev, width_in)
    field_re, field_im = rows_inverse(flat_re, flat_im, length, back_count)
    fields = field_re.reshape(5, ray_dev, length) * strength
    ray_tile = ray_state
    current = fields
    for step_index in range(HOPS):
        ray_tile = lens_step(ray_tile, current[None])
        if step_index + 1 < HOPS:
            current = shifted(current, "los", -1)
    ray_tile = shifted(ray_tile, "los", HOPS)
    return ray_tile


def solution(mesh):
    return jax.shard_map(
        per_device,
        mesh=mesh,
        in_specs=(
            P(("real", "los"), "sky", None),
            P(("real", "los")),
            P(("real", "los")),
            P(("real", "los"), None, "sky", None),
        ),
        out_specs=P(("real", "los"), None, "sky", None),
        check_vma=False,
    )
```

profile of v0, /device:TPU:0, one launch (start us, length us, event | category | flops | bytes accessed | tf_op | source)
XLA Modules:
  0.0 469.8 jit_solution(12532667981674408315)
XLA Ops:
  5.5 9.5 %fusion.217 = f32[16,1024,128]{2,0,1:T(8,128)} fusion(f32[1024,16,128]{2,1,0:T(8,128)S(1)} %bitcast.186), kind=kOutput, calls=%fused_computation.286 | convolution fusion | flops 402656768 | bytes 16777216 | tf_op jit(solution)/shard_map/rvu,vk->rku/dot_general | solution.py:77
  14.9 13.3 %subtract_bitcast_fusion = (f32[1024,16,128]{2,1,0:T(8,128)S(1)}, f32[1024,16,128]{2,1,0:T(8,128)S(1)}) fusion(f32[16,1024,128]{2,0,1:T(8,128)} %fusion.217, f32[16,128]{1,0:T(8,128)S(1)} %get-tuple-element.456, f32[16,128]{1,0:T(8,128)S(1)} %get-tuple-element.457, f32[1024,16,128]{2,1,0:T(8,128)} %bitcast.187), kind=kOutput, calls=%fused_computation.93 | convolution fusion | flops 415239680 | bytes 33570816 | tf_op jit(solution)/shard_map/rvu,vk->rku/dot_general | solution.py:77
  28.3 12.4 %fusion.71 = f32[1024,16,64]{0,2,1:T(8,128)S(1)} fusion(f32[1024,16,128]{2,1,0:T(8,128)S(1)} %get-tuple-element.442), kind=kOutput, calls=%fused_computation.96 | convolution fusion | flops 1610727424 | bytes 12582912 | tf_op jit(solution)/shard_map/rku,um->rkm/dot_general | solution.py:77
  40.7 14.0 %fusion.69 = f32[1024,16,64]{0,2,1:T(8,128)} fusion(f32[1024,16,128]{2,1,0:T(8,128)S(1)} %get-tuple-element.442), kind=kOutput, calls=%fused_computation.94 | convolution fusion | flops 1610727424 | bytes 12582912 | tf_op jit(solution)/shard_map/rku,um->rkm/dot_general | solution.py:77
  54.7 14.1 %fusion.105 = f32[1024,16,64]{0,2,1:T(8,128)} fusion(f32[1024,16,64]{0,2,1:T(8,128)S(1)} %fusion.71, f32[1024,16,128]{2,1,0:T(8,128)S(1)} %get-tuple-element.441), kind=kOutput, calls=%fused_computation.124 | convolution fusion | flops 1611776000 | bytes 16777216 | tf_op jit(solution)/shard_map/rku,um->rkm/dot_general | solution.py:77
  68.8 8.7 %copy.71 = f32[1,1024,1024]{1,0,2:T(1,128)} copy(f32[1,1024,1024]{1,2,0:T(8,128)} %bitcast.194) | data formatting | bytes 8388608 | tf_op jit(solution)/shard_map/stack;reshape | solution.py:244
  77.5 17.8 %fusion.108 = f32[1024,16,64]{0,2,1:T(8,128)} fusion(f32[1024,16,64]{0,2,1:T(8,128)S(1)} %copy-done.7, f32[1024,16,128]{2,1,0:T(8,128)} %copy-done.2), kind=kOutput, calls=%fused_computation.125 | convolution fusion | flops 1611776000 | bytes 16777216 | tf_op jit(solution)/shard_map/rku,um->rkm/dot_general | solution.py:77
  95.3 8.6 %copy.72 = f32[1,1024,1024]{1,0,2:T(1,128)} copy(f32[1,1024,1024]{1,2,0:T(8,128)} %bitcast.193) | data formatting | bytes 8388608 | tf_op jit(solution)/shard_map/stack;reshape | solution.py:244
  103.9 8.7 %pad_maximum_fusion.1 = f32[2,1024,1024]{1,0,2:T(2,128)S(1)} fusion(f32[1,1024,1024]{1,0,2:T(1,128)} %copy.72, f32[1,1024,1024]{1,0,2:T(1,128)S(1)} %copy-done.8), kind=kLoop, calls=%fused_computation.91 | loop fusion | flops 2097152 | bytes 16777216 | tf_op jit(solution)/shard_map/stack | solution.py:244
  112.6 10.6 %all_to_all.33 = f32[2,1024,1024]{1,0,2:T(2,128)S(1)} all-to-all(f32[2,1024,1024]{1,0,2:T(2,128)S(1)} %pad_maximum_fusion.1), channel_id=1, replica_groups=mesh['real'=2,'los'=8,'sky'=2] {'sky'}, dimensions={2} | all-to-all | bytes 16777216 | tf_op jit(solution)/shard_map/all_to_all | solution.py:243
  135.5 10.3 %fusion.87 = f32[64,32,512]{2,0,1:T(8,128)} fusion(f32[64,32,512]{2,1,0:T(8,128)} %bitcast.190), kind=kOutput, calls=%fused_computation.114 | convolution fusion | flops 805363712 | bytes 8388608 | tf_op jit(solution)/shard_map/abc,ak->kbc/dot_general | solution.py:77
  158.7 9.9 %fusion.93 = f32[64,32,512]{2,0,1:T(8,128)S(1)} fusion(f32[64,32,512]{2,0,1:T(8,128)} %fusion.87, f32[64,32,512]{2,1,0:T(8,128)} %bitcast.188), kind=kOutput, calls=%fused_computation.120 | convolution fusion | flops 806412288 | bytes 12582912 | tf_op jit(solution)/shard_map/abc,ak->kbc/dot_general | solution.py:77
  168.6 7.4 %multiply_subtract_fusion = (f32[64,32,512]{2,0,1:T(8,128)S(1)}, f32[64,32,512]{2,0,1:T(8,128)S(1)}) fusion(f32[64,32,512]{2,0,1:T(8,128)S(1)} %fusion.93, f32[64,32]{0,1:T(8,128)S(1)} %get-tuple-element.458, f32[64,32]{0,1:T(8,128)S(1)} %get-tuple-element.459, f32[64,32,512]{2,0,1:T(8,128)S(1)} %copy-done.6, f32[64,32,512]{2,1,0:T(8,128)S(1)} %bitcast.189), kind=kOutput, calls=%fused_computation.103 | convolution fusion | flops 812703744 | bytes 20987904 | tf_op jit(solution)/shard_map/abc,ak->kbc/dot_general | solution.py:77
  210.0 121.0 %while.19 = (s32[]{:T(128)}, f32[5,2,32,512]{3,1,0,2:T(2,128)S(1)}, s32[]{:T(128)}, f32[2048,512]{1,0:T(8,128)}, f32[2048,512]{1,0:T(8,128)}, /*index=5*/s32[32]...) while((s32[]{:T(128)}, f32[5,2,32,512]{3,1,0,2:T(2,128)S(1)}, ...), condition=%wide.region_1.2_spmd.clone.clone.clone, body=%wide.region_0.1_spmd.clone.clone.clone.sunk | while | flops 4079728128 | bytes 115730168 | solution.py:228
  249.1 7.2 %fusion.392 = f32[5,256,32]{1,2,0:T(8,128)S(1)} fusion(f32[5,2048,256]{2,1,0:T(8,128)S(1)} %get-tuple-element.513, s32[32]{0:T(128)S(1)} %get-tuple-element.540), kind=kOutput, calls=%fused_computation.43.clone.1 | convolution fusion | flops 1007550464 | bytes 10649728 | tf_op jit(solution)/shard_map/while/body/eval_jaxpr/fkc,rk->frc/dot_general | solution.py:77
  256.3 7.2 %fusion.393 = f32[5,1,32,256]{3,2,0,1:T(8,128)S(1)} fusion(f32[5,256,32]{1,2,0:T(8,128)S(1)} %fusion.392, f32[5,2048,256]{2,1,0:T(8,128)S(1)} %bitcast_dynamic-update-slice_fusion.25, s32[32]{0:T(128)S(1)} %get-tuple-element.540), kind=kOutput, calls=%fused_computation.30.clone.1 | convolution fusion | flops 1007591424 | bytes 10813568 | tf_op jit(solution)/shard_map/while/body/eval_jaxpr/fkc,rk->frc/dot_general | solution.py:77
  270.7 7.2 %fusion.391 = f32[5,1,32,256]{3,2,0,1:T(8,128)S(1)} fusion(f32[5,256,32]{1,2,0:T(8,128)S(1)} %fusion.390, f32[5,2048,256]{2,1,0:T(8,128)S(1)} %bitcast_dynamic-update-slice_fusion.25, s32[32]{0:T(128)S(1)} %get-tuple-element.540), kind=kOutput, calls=%fused_computation.28.clone.1 | convolution fusion | flops 1007591424 | bytes 10813568 | tf_op jit(solution)/shard_map/while/body/eval_jaxpr/fkc,rk->frc/dot_general | solution.py:77
  295.7 7.2 %fusion.392 = f32[5,256,32]{1,2,0:T(8,128)S(1)} fusion(f32[5,2048,256]{2,1,0:T(8,128)S(1)} %get-tuple-element.513, s32[32]{0:T(128)S(1)} %get-tuple-element.540), kind=kOutput, calls=%fused_computation.43.clone.1 | convolution fusion | flops 1007550464 | bytes 10649728 | tf_op jit(solution)/shard_map/while/body/eval_jaxpr/fkc,rk->frc/dot_general | solution.py:77
  302.9 7.2 %fusion.393 = f32[5,1,32,256]{3,2,0,1:T(8,128)S(1)} fusion(f32[5,256,32]{1,2,0:T(8,128)S(1)} %fusion.392, f32[5,2048,256]{2,1,0:T(8,128)S(1)} %bitcast_dynamic-update-slice_fusion.25, s32[32]{0:T(128)S(1)} %get-tuple-element.540), kind=kOutput, calls=%fused_computation.30.clone.1 | convolution fusion | flops 1007591424 | bytes 10813568 | tf_op jit(solution)/shard_map/while/body/eval_jaxpr/fkc,rk->frc/dot_general | solution.py:77
  317.3 7.2 %fusion.391 = f32[5,1,32,256]{3,2,0,1:T(8,128)S(1)} fusion(f32[5,256,32]{1,2,0:T(8,128)S(1)} %fusion.390, f32[5,2048,256]{2,1,0:T(8,128)S(1)} %bitcast_dynamic-update-slice_fusion.25, s32[32]{0:T(128)S(1)} %get-tuple-element.540), kind=kOutput, calls=%fused_computation.28.clone.1 | convolution fusion | flops 1007591424 | bytes 10813568 | tf_op jit(solution)/shard_map/while/body/eval_jaxpr/fkc,rk->frc/dot_general | solution.py:77
  349.8 14.5 %collective-permute-done = f32[5,16,2048]{2,1,0:T(8,128)S(1)} collective-permute-done((f32[5,16,2048]{2,1,0:T(8,128)}, f32[5,16,2048]{2,1,0:T(8,128)S(1)}, u32[]{:S(2)}, u32[]{:S(2)}) %collective-permute-start) | collective-permute-done | bytes 655392 | tf_op jit(solution)/shard_map/ppermute | solution.py:16
  369.6 13.2 %collective-permute-done.1 = f32[5,16,2048]{2,1,0:T(8,128)S(1)} collective-permute-done((f32[5,16,2048]{2,1,0:T(8,128)S(1)}, f32[5,16,2048]{2,1,0:T(8,128)S(1)}, u32[]{:S(2)}, u32[]{:S(2)}) %collective-permute-start.1) | collective-permute-done | bytes 655392 | tf_op jit(solution)/shard_map/ppermute | solution.py:16
  388.2 13.9 %collective-permute-done.2 = f32[5,16,2048]{2,1,0:T(8,128)S(1)} collective-permute-done((f32[5,16,2048]{2,1,0:T(8,128)S(1)}, f32[5,16,2048]{2,1,0:T(8,128)S(1)}, u32[]{:S(2)}, u32[]{:S(2)}) %collective-permute-start.2) | collective-permute-done | bytes 655392 | tf_op jit(solution)/shard_map/ppermute | solution.py:16
  402.7 65.7 %collective-permute-done.3 = f32[1,12,16,2048]{3,2,1,0:T(8,128)S(1)} collective-permute-done((f32[1,12,16,2048]{3,2,1,0:T(8,128)S(1)}, f32[1,12,16,2048]{3,2,1,0:T(8,128)S(1)}, u32[]{:S(2)}, u32[]{:S(2)}) %collective-permute-start.3) | collective-permute-done | bytes 1572896 | tf_op jit(solution)/shard_map/ppermute | solution.py:16
  (116 shorter events, 143.7 us)
Async XLA Ops:
  5.5 9.5 %copy-start.3 = (f32[128,8,16,128]{3,2,1,0:T(8,128)}, f32[128,8,16,128]{3,2,1,0:T(8,128)S(1)}, u32[]{:S(2)}) copy-start(f32[128,8,16,128]{3,2,1,0:T(8,128)S(1)} %copy.90) | copy-start | bytes 25165828
  28.3 26.4 %copy-start.2 = (f32[1024,16,128]{2,1,0:T(8,128)}, f32[1024,16,128]{2,1,0:T(8,128)S(1)}, u32[]{:S(2)}) copy-start(f32[1024,16,128]{2,1,0:T(8,128)S(1)} %get-tuple-element.441) | copy-start | bytes 25165828
  68.8 8.7 %copy-start.7 = (f32[1024,16,64]{0,2,1:T(8,128)S(1)}, f32[1024,16,64]{0,2,1:T(8,128)}, u32[]{:S(2)}) copy-start(f32[1024,16,64]{0,2,1:T(8,128)} %fusion.69) | copy-start | bytes 12582916
  95.3 8.6 %copy-start.8 = (f32[1,1024,1024]{1,0,2:T(1,128)S(1)}, f32[1,1024,1024]{1,0,2:T(1,128)}, u32[]{:S(2)}) copy-start(f32[1,1024,1024]{1,0,2:T(1,128)} %copy.71) | copy-start | bytes 12582916
  135.5 10.3 %copy-start.5 = (f32[1,2,1024,512]{3,2,1,0:T(8,128)S(1)}, f32[1,2,1024,512]{3,2,1,0:T(8,128)}, u32[]{:S(2)}) copy-start(f32[1,2,1024,512]{3,2,1,0:T(8,128)} %copy.76) | copy-start | bytes 12582916
  158.7 9.9 %copy-start.4 = (f32[1,2,1024,512]{3,2,1,0:T(8,128)S(1)}, f32[1,2,1024,512]{3,2,1,0:T(8,128)}, u32[]{:S(2)}) copy-start(f32[1,2,1024,512]{3,2,1,0:T(8,128)} %copy.74) | copy-start | bytes 12582916
  158.7 9.9 %copy-start.6 = (f32[64,32,512]{2,0,1:T(8,128)S(1)}, f32[64,32,512]{2,0,1:T(8,128)}, u32[]{:S(2)}) copy-start(f32[64,32,512]{2,0,1:T(8,128)} %fusion.85) | copy-start | bytes 12582916
  232.0 3.5 copy-start
  235.5 2.2 copy-start.1
  278.4 3.5 copy-start
  281.9 2.2 copy-start.1
  342.0 27.4 %copy-start.9 = (f32[1,12,16,2048]{3,2,1,0:T(8,128)S(1)}, f32[1,12,16,2048]{3,2,1,0:T(8,128)}, u32[]{:S(2)}) copy-start(f32[1,12,16,2048]{3,2,1,0:T(8,128)} %param.9) | copy-start | bytes 4718596
  343.7 20.6 %collective-permute-start = (f32[5,16,2048]{2,1,0:T(8,128)}, f32[5,16,2048]{2,1,0:T(8,128)S(1)}, u32[]{:S(2)}, u32[]{:S(2)}) collective-permute-start(f32[5,16,2048]{2,1,0:T(8,128)} %mul.1716), channel_id=1, source_target_pairs={{2,0},{4,2},{6,4},{8,6},{10,8},{12,10},{14,12},{0,14},{3,1},{5,3},... | collective-permute-start | bytes 1966088 | tf_op jit(solution)/shard_map/ppermute | solution.py:16
  364.3 18.5 %collective-permute-start.1 = (f32[5,16,2048]{2,1,0:T(8,128)S(1)}, f32[5,16,2048]{2,1,0:T(8,128)S(1)}, u32[]{:S(2)}, u32[]{:S(2)}) collective-permute-start(f32[5,16,2048]{2,1,0:T(8,128)S(1)} %collective-permute-done), channel_id=1, source_target_pairs={{2,0},{4,2},{6,4},{8,6},{10,8},{12,10},{14,12},{0,14},{3,1},{5,3},... | collective-permute-start | bytes 1966088 | tf_op jit(solution)/shard_map/ppermute | solution.py:16
  382.9 19.3 %collective-permute-start.2 = (f32[5,16,2048]{2,1,0:T(8,128)S(1)}, f32[5,16,2048]{2,1,0:T(8,128)S(1)}, u32[]{:S(2)}, u32[]{:S(2)}) collective-permute-start(f32[5,16,2048]{2,1,0:T(8,128)S(1)} %collective-permute-done.1), channel_id=1, source_target_pairs={{2,0},{4,2},{6,4},{8,6},{10,8},{12,10},{14,12},{0,14},{3,1},{5,3},... | collective-permute-start | bytes 1966088 | tf_op jit(solution)/shard_map/ppermute | solution.py:16
  402.6 65.8 %collective-permute-start.3 = (f32[1,12,16,2048]{3,2,1,0:T(8,128)S(1)}, f32[1,12,16,2048]{3,2,1,0:T(8,128)S(1)}, u32[]{:S(2)}, u32[]{:S(2)}) collective-permute-start(f32[1,12,16,2048]{3,2,1,0:T(8,128)S(1)} %constant_dynamic-update-slice_fusion), channel_id=1, source_target_pairs={{8,0},{10,2},{12,4},{14,6},{0,8},{2,10},{4,12},{6,14},{9,1},{11,3}... | collective-permute-start | bytes 4718600 | tf_op jit(solution)/shard_map/ppermute | solution.py:16
where the time goes:
time: 478 us; the launch traced here: 470 us
  matrix products  203 us (42%)
  waiting for transfers between devices  107 us (22%)
  local copies, waits for them, and re-layouts  54.4 us (11%)
  other arithmetic  43.8 us (9%)
  loops' own time  28.4 us (6%)
  starting transfers between devices  16.3 us (3%)
  blocking collectives  14.9 us (3%)
    dot_general x28, matrix products, mixed(): jnp.einsum(form, left_op, right_op, precision=highest, preferred_element_...  203 us
    ppermute x4, waiting for transfers between devices, shifted(): return lax.ppermute(block, axis, route)  107 us
    while x14, other arithmetic  29.8 us
    another operation x1, loops' own time, spectral_rows(): return lax.fori_loop(0, blocks, one_block, initial)  28.4 us
    another operation x2, local copies, waits for them, and re-layouts, per_device(): jnp.stack([row_re, row_im])  17.3 us
    ppermute x4, starting transfers between devices, shifted(): return lax.ppermute(block, axis, route)  16.3 us
    slice x3, local copies, waits for them, and re-layouts, per_device(): spec_re, spec_im = transform_first(spread[0], spread[1], -1.0)  15.3 us
    all_to_all x1, blocking collectives, per_device(): lax.all_to_all(jnp.stack([row_re, row_im]), 'sky', split_axis=2, concat_a...  10.6 us
  transfers between devices with their start and end apart: 4, of which 4 were waited for; matrix products, arithmetic and copies ran while one was open for 0% of the time, Pallas kernels for 0%

commit v1 on v0

--- a/solution.py
+++ b/solution.py
@@ -8,6 +8,12 @@
 two_pi = 2.0 * math.pi
 highest = lax.Precision.HIGHEST
 first_radix = 16
+pack_rows_here = lambda frame, dim_no, k_dim: jnp.concatenate(
+    jax.lax.all_to_all(
+        jnp.stack(jnp.split(frame, jax.lax.axis_size("sky"), axis=dim_no)), "sky", 0, 0
+    ),
+    axis=k_dim,
+)
 
 
 def shifted(block, axis, distance):
@@ -240,9 +246,7 @@
     strength = lens_weight[0] * plane_count[0].astype(jnp.float32)
     back_count = second // 2
     row_re, row_im = rows_forward(plane_cells, first_radix, back_count)
-    spread = lax.all_to_all(
-        jnp.stack([row_re, row_im]), "sky", split_axis=2, concat_axis=1, tiled=True
-    )
+    spread = pack_rows_here(jnp.stack([row_re, row_im]), 2, 1)
     spec_re, spec_im = transform_first(spread[0], spread[1], -1.0)
     half_count = length // (2 * sky_count)
     packed = spectral_rows(

time: 478 us -> 450 us (0.941)
  local copies, waits for them, and re-layouts: 54.4 us -> 35 us
  matrix products: 203 us -> 196 us
    slice x3 -> x1, local copies, waits for them, and re-layouts: 15.3 us -> 0.98 us  [per_device(): spec_re, spec_im = transform_first(spread[0], spread[1], -1.0)]
    dot_general x28, matrix products: 203 us -> 196 us  [mixed(): jnp.einsum(form, left_op, right_op, precision=highest, preferred_element_...]
    another operation x2, local copies, waits for them, and re-layouts: 17.3 us -> 10.9 us  [per_device(): spread = pack_rows_here(jnp.stack([row_re, row_im]), 2, 1)]
where the time goes in v1:
time: 450 us; the launch traced here: 442 us
  matrix products  196 us (44%)
  waiting for transfers between devices  107 us (24%)
  other arithmetic  41.5 us (9%)
  local copies, waits for them, and re-layouts  35 us (8%)
  loops' own time  28.3 us (6%)
  starting transfers between devices  16.3 us (4%)
  blocking collectives  16.1 us (4%)
    dot_general x28, matrix products, mixed(): jnp.einsum(form, left_op, right_op, precision=highest, preferred_element_...  196 us
    ppermute x4, waiting for transfers between devices, shifted(): return lax.ppermute(block, axis, route)  107 us
    while x14, other arithmetic  31.4 us
    another operation x1, loops' own time, spectral_rows(): return lax.fori_loop(0, blocks, one_block, initial)  28.3 us
    ppermute x4, starting transfers between devices, shifted(): return lax.ppermute(block, axis, route)  16.3 us
    all_to_all x1, blocking collectives, jax.lax.all_to_all(jnp.stack(jnp.split(frame, jax.lax.axis_size('sky'), a...  11.8 us
    another operation x2, local copies, waits for them, and re-layouts, per_device(): spread = pack_rows_here(jnp.stack([row_re, row_im]), 2, 1)  10.9 us
  transfers between devices with their start and end apart: 4, of which 4 were waited for; matrix products, arithmetic and copies ran while one was open for 0% of the time, Pallas kernels for 0%

profile of v1, /device:TPU:0, one launch (start us, length us, event | category | flops | bytes accessed | tf_op | source)
XLA Modules:
  0.0 441.9 jit_solution(5276548206694269788)
XLA Ops:
  5.5 9.5 %fusion.220 = f32[16,1024,128]{2,0,1:T(8,128)} fusion(f32[1024,16,128]{2,1,0:T(8,128)S(1)} %bitcast.190), kind=kOutput, calls=%fused_computation.293 | convolution fusion | flops 402656768 | bytes 16777216 | tf_op jit(solution)/shard_map/rvu,vk->rku/dot_general | solution.py:83
  14.9 13.3 %subtract_bitcast_fusion = (f32[1024,16,128]{2,1,0:T(8,128)S(1)}, f32[1024,16,128]{2,1,0:T(8,128)S(1)}) fusion(f32[16,1024,128]{2,0,1:T(8,128)} %fusion.220, f32[16,128]{1,0:T(8,128)S(1)} %get-tuple-element.458, f32[16,128]{1,0:T(8,128)S(1)} %get-tuple-element.459, f32[1024,16,128]{2,1,0:T(8,128)} %bitcast.191), kind=kOutput, calls=%fused_computation.96 | convolution fusion | flops 415239680 | bytes 33570816 | tf_op jit(solution)/shard_map/rvu,vk->rku/dot_general | solution.py:83
  28.3 12.4 %fusion.69 = f32[1024,16,64]{0,2,1:T(8,128)S(1)} fusion(f32[1024,16,128]{2,1,0:T(8,128)S(1)} %get-tuple-element.442), kind=kOutput, calls=%fused_computation.97 | convolution fusion | flops 1610727424 | bytes 12582912 | tf_op jit(solution)/shard_map/rku,um->rkm/dot_general | solution.py:83
  40.7 14.1 %fusion.71 = f32[1024,16,64]{0,2,1:T(8,128)} fusion(f32[1024,16,128]{2,1,0:T(8,128)S(1)} %get-tuple-element.442), kind=kOutput, calls=%fused_computation.99 | convolution fusion | flops 1610727424 | bytes 12582912 | tf_op jit(solution)/shard_map/rku,um->rkm/dot_general | solution.py:83
  54.8 14.0 %fusion.111 = f32[1024,16,64]{0,2,1:T(8,128)} fusion(f32[1024,16,64]{0,2,1:T(8,128)S(1)} %fusion.69, f32[1024,16,128]{2,1,0:T(8,128)S(1)} %get-tuple-element.441), kind=kOutput, calls=%fused_computation.132 | convolution fusion | flops 1611776000 | bytes 16777216 | tf_op jit(solution)/shard_map/rku,um->rkm/dot_general | solution.py:83
  74.3 18.5 %fusion.108 = f32[1024,16,64]{0,2,1:T(8,128)} fusion(f32[1024,16,64]{0,2,1:T(8,128)} %fusion.71, f32[1024,16,128]{2,1,0:T(8,128)} %copy-done.2), kind=kOutput, calls=%fused_computation.131 | convolution fusion | flops 1611776000 | bytes 16777216 | tf_op jit(solution)/shard_map/rku,um->rkm/dot_general | solution.py:83
  103.0 11.8 %all_to_all.23 = f32[2,2,1024,512]{3,2,1,0:T(8,128)} all-to-all(f32[2,2,1024,512]{3,2,1,0:T(8,128)S(1)} %pad_maximum_fusion.1), channel_id=1, replica_groups=mesh['real'=2,'los'=8,'sky'=2] {'sky'}, dimensions={0} | all-to-all | bytes 16777216 | tf_op jit(solution)/shard_map/all_to_all | solution.py:12
  126.3 6.5 %fusion.88 = f32[64,32,512]{2,0,1:T(8,128)S(1)} fusion(f32[64,32,512]{2,1,0:T(8,128)S(1)} %bitcast.195), kind=kOutput, calls=%fused_computation.119 | convolution fusion | flops 805363712 | bytes 8388608 | tf_op jit(solution)/shard_map/abc,ak->kbc/dot_general | solution.py:83
  132.9 6.5 %fusion.96 = f32[64,32,512]{2,0,1:T(8,128)S(1)} fusion(f32[64,32,512]{2,0,1:T(8,128)S(1)} %fusion.90, f32[64,32,512]{2,1,0:T(8,128)S(1)} %bitcast.192), kind=kOutput, calls=%fused_computation.127 | convolution fusion | flops 806412288 | bytes 12582912 | tf_op jit(solution)/shard_map/abc,ak->kbc/dot_general | solution.py:83
  139.4 7.5 %multiply_subtract_fusion = (f32[64,32,512]{2,0,1:T(8,128)S(1)}, f32[64,32,512]{2,0,1:T(8,128)S(1)}) fusion(f32[64,32,512]{2,0,1:T(8,128)S(1)} %fusion.96, f32[64,32]{0,1:T(8,128)S(1)} %get-tuple-element.460, f32[64,32]{0,1:T(8,128)S(1)} %get-tuple-element.461, f32[64,32,512]{2,0,1:T(8,128)S(1)} %fusion.88, f32[64,32,512]{2,1,0:T(8,128)S(1)} %bitcast.193), kind=kOutput, calls=%fused_computation.110 | convolution fusion | flops 812703744 | bytes 20987904 | tf_op jit(solution)/shard_map/abc,ak->kbc/dot_general | solution.py:83
  170.1 6.4 %fusion.102 = f32[32,64,512]{2,0,1:T(8,128)S(1)} fusion(f32[32,64,512]{2,0,1:T(8,128)S(1)} %fusion.82, f32[64,32,512]{2,0,1:T(8,128)S(1)} %get-tuple-element.443), kind=kOutput, calls=%fused_computation.129 | convolution fusion | flops 403716096 | bytes 12582912 | tf_op jit(solution)/shard_map/kbc,bm->mkc/dot_general | solution.py:83
  181.1 122.0 %while.19 = (s32[]{:T(128)}, f32[5,2,32,512]{3,1,0,2:T(2,128)S(1)}, s32[]{:T(128)}, f32[2048,512]{1,0:T(8,128)}, f32[2048,512]{1,0:T(8,128)}, /*index=5*/s32[32]...) while((s32[]{:T(128)}, f32[5,2,32,512]{3,1,0,2:T(2,128)S(1)}, ...), condition=%wide.region_1.2_spmd.clone.clone.clone, body=%wide.region_0.1_spmd.clone.clone.clone.sunk | while | flops 4079728128 | bytes 115730168 | solution.py:234
  220.7 7.2 %fusion.395 = f32[5,256,32]{1,2,0:T(8,128)S(1)} fusion(f32[5,2048,256]{2,1,0:T(8,128)S(1)} %get-tuple-element.515, s32[32]{0:T(128)S(1)} %get-tuple-element.542), kind=kOutput, calls=%fused_computation.43.clone.1 | convolution fusion | flops 1007550464 | bytes 10649728 | tf_op jit(solution)/shard_map/while/body/eval_jaxpr/fkc,rk->frc/dot_general | solution.py:83
  227.9 7.2 %fusion.396 = f32[5,1,32,256]{3,2,0,1:T(8,128)S(1)} fusion(f32[5,256,32]{1,2,0:T(8,128)S(1)} %fusion.395, f32[5,2048,256]{2,1,0:T(8,128)S(1)} %bitcast_dynamic-update-slice_fusion.25, s32[32]{0:T(128)S(1)} %get-tuple-element.542), kind=kOutput, calls=%fused_computation.30.clone.1 | convolution fusion | flops 1007591424 | bytes 10813568 | tf_op jit(solution)/shard_map/while/body/eval_jaxpr/fkc,rk->frc/dot_general | solution.py:83
  235.1 7.2 %fusion.393 = f32[5,256,32]{1,2,0:T(8,128)S(1)} fusion(f32[5,2048,256]{2,1,0:T(8,128)S(1)} %get-tuple-element.515, s32[32]{0:T(128)S(1)} %get-tuple-element.542), kind=kOutput, calls=%fused_computation.39.clone.1 | convolution fusion | flops 1007550464 | bytes 10649728 | tf_op jit(solution)/shard_map/while/body/eval_jaxpr/fkc,rk->frc/dot_general | solution.py:83
  242.3 7.2 %fusion.394 = f32[5,1,32,256]{3,2,0,1:T(8,128)S(1)} fusion(f32[5,256,32]{1,2,0:T(8,128)S(1)} %fusion.393, f32[5,2048,256]{2,1,0:T(8,128)S(1)} %bitcast_dynamic-update-slice_fusion.25, s32[32]{0:T(128)S(1)} %get-tuple-element.542), kind=kOutput, calls=%fused_computation.28.clone.1 | convolution fusion | flops 1007591424 | bytes 10813568 | tf_op jit(solution)/shard_map/while/body/eval_jaxpr/fkc,rk->frc/dot_general | solution.py:83
  267.9 7.2 %fusion.395 = f32[5,256,32]{1,2,0:T(8,128)S(1)} fusion(f32[5,2048,256]{2,1,0:T(8,128)S(1)} %get-tuple-element.515, s32[32]{0:T(128)S(1)} %get-tuple-element.542), kind=kOutput, calls=%fused_computation.43.clone.1 | convolution fusion | flops 1007550464 | bytes 10649728 | tf_op jit(solution)/shard_map/while/body/eval_jaxpr/fkc,rk->frc/dot_general | solution.py:83
  275.1 7.2 %fusion.396 = f32[5,1,32,256]{3,2,0,1:T(8,128)S(1)} fusion(f32[5,256,32]{1,2,0:T(8,128)S(1)} %fusion.395, f32[5,2048,256]{2,1,0:T(8,128)S(1)} %bitcast_dynamic-update-slice_fusion.25, s32[32]{0:T(128)S(1)} %get-tuple-element.542), kind=kOutput, calls=%fused_computation.30.clone.1 | convolution fusion | flops 1007591424 | bytes 10813568 | tf_op jit(solution)/shard_map/while/body/eval_jaxpr/fkc,rk->frc/dot_general | solution.py:83
  282.3 7.2 %fusion.393 = f32[5,256,32]{1,2,0:T(8,128)S(1)} fusion(f32[5,2048,256]{2,1,0:T(8,128)S(1)} %get-tuple-element.515, s32[32]{0:T(128)S(1)} %get-tuple-element.542), kind=kOutput, calls=%fused_computation.39.clone.1 | convolution fusion | flops 1007550464 | bytes 10649728 | tf_op jit(solution)/shard_map/while/body/eval_jaxpr/fkc,rk->frc/dot_general | solution.py:83
  289.5 7.2 %fusion.394 = f32[5,1,32,256]{3,2,0,1:T(8,128)S(1)} fusion(f32[5,256,32]{1,2,0:T(8,128)S(1)} %fusion.393, f32[5,2048,256]{2,1,0:T(8,128)S(1)} %bitcast_dynamic-update-slice_fusion.25, s32[32]{0:T(128)S(1)} %get-tuple-element.542), kind=kOutput, calls=%fused_computation.28.clone.1 | convolution fusion | flops 1007591424 | bytes 10813568 | tf_op jit(solution)/shard_map/while/body/eval_jaxpr/fkc,rk->frc/dot_general | solution.py:83
  322.0 14.5 %collective-permute-done = f32[5,16,2048]{2,1,0:T(8,128)S(1)} collective-permute-done((f32[5,16,2048]{2,1,0:T(8,128)}, f32[5,16,2048]{2,1,0:T(8,128)S(1)}, u32[]{:S(2)}, u32[]{:S(2)}) %collective-permute-start) | collective-permute-done | bytes 655392 | tf_op jit(solution)/shard_map/ppermute | solution.py:22
  341.8 13.2 %collective-permute-done.1 = f32[5,16,2048]{2,1,0:T(8,128)S(1)} collective-permute-done((f32[5,16,2048]{2,1,0:T(8,128)S(1)}, f32[5,16,2048]{2,1,0:T(8,128)S(1)}, u32[]{:S(2)}, u32[]{:S(2)}) %collective-permute-start.1) | collective-permute-done | bytes 655392 | tf_op jit(solution)/shard_map/ppermute | solution.py:22
  360.4 13.9 %collective-permute-done.2 = f32[5,16,2048]{2,1,0:T(8,128)S(1)} collective-permute-done((f32[5,16,2048]{2,1,0:T(8,128)S(1)}, f32[5,16,2048]{2,1,0:T(8,128)S(1)}, u32[]{:S(2)}, u32[]{:S(2)}) %collective-permute-start.2) | collective-permute-done | bytes 655392 | tf_op jit(solution)/shard_map/ppermute | solution.py:22
  374.9 65.7 %collective-permute-done.3 = f32[1,12,16,2048]{3,2,1,0:T(8,128)S(1)} collective-permute-done((f32[1,12,16,2048]{3,2,1,0:T(8,128)S(1)}, f32[1,12,16,2048]{3,2,1,0:T(8,128)S(1)}, u32[]{:S(2)}, u32[]{:S(2)}) %collective-permute-start.3) | collective-permute-done | bytes 1572896 | tf_op jit(solution)/shard_map/ppermute | solution.py:22
  (105 shorter events, 126.5 us)
Async XLA Ops:
  5.5 9.5 %copy-start.3 = (f32[128,8,16,128]{3,2,1,0:T(8,128)}, f32[128,8,16,128]{3,2,1,0:T(8,128)S(1)}, u32[]{:S(2)}) copy-start(f32[128,8,16,128]{3,2,1,0:T(8,128)S(1)} %copy.72) | copy-start | bytes 25165828
  28.3 26.5 %copy-start.2 = (f32[1024,16,128]{2,1,0:T(8,128)}, f32[1024,16,128]{2,1,0:T(8,128)S(1)}, u32[]{:S(2)}) copy-start(f32[1024,16,128]{2,1,0:T(8,128)S(1)} %get-tuple-element.441) | copy-start | bytes 25165828
  202.9 4.4 copy-start
  203.0 6.3 %copy-start.1 = (f32[2048,512]{1,0:T(8,128)S(1)}, f32[2048,512]{1,0:T(8,128)}, u32[]{:S(2)}) copy-start(f32[2048,512]{1,0:T(8,128)} %get-tuple-element.541) | copy-start | bytes 12582916 | tf_op jit(solution)/shard_map/while
  249.9 4.4 copy-start
  250.0 6.3 %copy-start.1 = (f32[2048,512]{1,0:T(8,128)S(1)}, f32[2048,512]{1,0:T(8,128)}, u32[]{:S(2)}) copy-start(f32[2048,512]{1,0:T(8,128)} %get-tuple-element.541) | copy-start | bytes 12582916 | tf_op jit(solution)/shard_map/while
  311.4 30.2 %copy-start.4 = (f32[1,12,16,2048]{3,2,1,0:T(8,128)S(1)}, f32[1,12,16,2048]{3,2,1,0:T(8,128)}, u32[]{:S(2)}) copy-start(f32[1,12,16,2048]{3,2,1,0:T(8,128)} %param.9) | copy-start | bytes 4718596
  315.9 20.6 %collective-permute-start = (f32[5,16,2048]{2,1,0:T(8,128)}, f32[5,16,2048]{2,1,0:T(8,128)S(1)}, u32[]{:S(2)}, u32[]{:S(2)}) collective-permute-start(f32[5,16,2048]{2,1,0:T(8,128)} %mul.1716), channel_id=1, source_target_pairs={{2,0},{4,2},{6,4},{8,6},{10,8},{12,10},{14,12},{0,14},{3,1},{5,3},... | collective-permute-start | bytes 1966088 | tf_op jit(solution)/shard_map/ppermute | solution.py:22
  336.5 18.5 %collective-permute-start.1 = (f32[5,16,2048]{2,1,0:T(8,128)S(1)}, f32[5,16,2048]{2,1,0:T(8,128)S(1)}, u32[]{:S(2)}, u32[]{:S(2)}) collective-permute-start(f32[5,16,2048]{2,1,0:T(8,128)S(1)} %collective-permute-done), channel_id=1, source_target_pairs={{2,0},{4,2},{6,4},{8,6},{10,8},{12,10},{14,12},{0,14},{3,1},{5,3},... | collective-permute-start | bytes 1966088 | tf_op jit(solution)/shard_map/ppermute | solution.py:22
  355.0 19.3 %collective-permute-start.2 = (f32[5,16,2048]{2,1,0:T(8,128)S(1)}, f32[5,16,2048]{2,1,0:T(8,128)S(1)}, u32[]{:S(2)}, u32[]{:S(2)}) collective-permute-start(f32[5,16,2048]{2,1,0:T(8,128)S(1)} %collective-permute-done.1), channel_id=1, source_target_pairs={{2,0},{4,2},{6,4},{8,6},{10,8},{12,10},{14,12},{0,14},{3,1},{5,3},... | collective-permute-start | bytes 1966088 | tf_op jit(solution)/shard_map/ppermute | solution.py:22
  374.8 65.8 %collective-permute-start.3 = (f32[1,12,16,2048]{3,2,1,0:T(8,128)S(1)}, f32[1,12,16,2048]{3,2,1,0:T(8,128)S(1)}, u32[]{:S(2)}, u32[]{:S(2)}) collective-permute-start(f32[1,12,16,2048]{3,2,1,0:T(8,128)S(1)} %constant_dynamic-update-slice_fusion), channel_id=1, source_target_pairs={{8,0},{10,2},{12,4},{14,6},{0,8},{2,10},{4,12},{6,14},{9,1},{11,3}... | collective-permute-start | bytes 4718600 | tf_op jit(solution)/shard_map/ppermute | solution.py:22
